TPU v7x, 32 devices: a whole 2x2x4 slice. The times are simulated.
32 devices in a mesh: dp: 8 (over z, y), tensor: 4 (over x, core).
Axes of the slice: x: 2, y: 2, z: 4, core: 2. Of those that a mesh axis runs over, the one named last changes fastest.
Arguments:
- pre_hidden: bfloat16 [8192, 2048], P(('dp', 'tensor')), may hold values from -6 to 6
- dec_hidden: bfloat16 [16, 2048], P('dp'), may hold values from -6 to 6
- norm_gain: bfloat16 [2048], replicated, may hold values from 0.5 to 1.5
- norm_shift: bfloat16 [2048], replicated, may hold values from -3 to 3
- qkv_weight: bfloat16 [2048, 6144], P(None, 'tensor'), may hold values from -0.125 to 0.125
- qkv_bias: bfloat16 [6144], P('tensor'), may hold values from -3 to 3
- out_weight: bfloat16 [2048, 2048], P('tensor'), may hold values from -0.125 to 0.125
- out_bias: bfloat16 [2048], replicated, may hold values from -3 to 3
- pre_keys: bfloat16 [8, 1024, 2048], P('dp', None, 'tensor'), may hold values from -480 to 480
- pre_values: bfloat16 [8, 1024, 2048], P('dp', None, 'tensor'), may hold values from -6 to 6
- dec_keys: bfloat16 [16, 2048, 2048], P('dp', None, 'tensor'), may hold values from -480 to 480
- dec_values: bfloat16 [16, 2048, 2048], P('dp', None, 'tensor'), may hold values from -6 to 6
- prefix_lengths: int32 [8], P('dp'), may hold values from 0 to 1024, as said below
- cache_lengths: int32 [16], P('dp'), may hold values from 1 to 2048, as said below
- slot_of: int32 [16], replicated, may hold values from 0 to 15, each once
Outputs:
- pre_output: bfloat16 [8192, 2048], P(('dp', 'tensor'))
- dec_output: bfloat16 [16, 2048], P('dp')
Inputs may be any that keep to these rules, and one draw needn't show every extreme that they name: `slot_of`: each decode slot is used by exactly one decode request. `prefix_lengths`: the longest prefix equals 1024. `cache_lengths`: the longest decode cache equals 2048.
All inputs are finite; a program needn't handle non-finite values.
Results may differ from a plain program's by a relative error of at most 0.0049.
The roundings to bfloat16 on the way count: a program that leaves them out, or rounds other values in their place, can miss the bound.
Values may be sent and summed in bfloat16 or wider, within the bound.
No kernel may reach another device: no remote copies, remote signals or barrier semaphores. Data moves between devices by JAX's collectives and lax.ppermute only.
A program may use at most 128 MiB of HBM per device.

v0:
```python
import math
import jax
import jax.numpy as jnp
from jax import lax
from jax.sharding import PartitionSpec as P

H = 16
HD = 128
EPSILON = 1e-05


def normalize(values, norm_gain, norm_shift):
    values = values.astype(jnp.float32)
    center = values - jnp.mean(values, axis=-1, keepdims=True)
    spread = jnp.mean(center * center, axis=-1, keepdims=True)
    scaled = center * lax.rsqrt(spread + EPSILON)
    return (scaled * norm_gain.astype(jnp.float32) + norm_shift.astype(jnp.float32)).astype(
        jnp.bfloat16
    )


def alibi_slopes(first_head, head_count, total_heads):
    head_ids = (first_head + jnp.arange(head_count, dtype=jnp.int32)).astype(jnp.float32)
    return jnp.exp2(-8.0 * (head_ids + 1.0) / total_heads)


def prefill_attention(merged_rows, cache_keys, cache_values, prefix, slopes):
    queries = merged_rows[:, :, 0]
    new_keys = merged_rows[:, :, 1]
    new_values = merged_rows[:, :, 2]
    group_size = merged_rows.shape[0]
    cache_size = cache_keys.shape[0]
    factor = 1.0 / math.sqrt(merged_rows.shape[-1])
    query_pos = prefix + jnp.arange(group_size, dtype=jnp.int32)
    cache_pos = jnp.arange(cache_size, dtype=jnp.int32)
    cache_dist = (query_pos[:, None] - cache_pos[None, :]).astype(jnp.float32)
    new_dist = (query_pos[:, None] - query_pos[None, :]).astype(jnp.float32)
    cache_scores = (
        jnp.einsum("qhd,khd->hqk", queries, cache_keys, preferred_element_type=jnp.float32) * factor
    )
    cache_scores = cache_scores - slopes[:, None, None] * cache_dist[None]
    cache_scores = jnp.where((cache_pos < prefix)[None, None, :], cache_scores, -jnp.inf)
    new_scores = (
        jnp.einsum("qhd,khd->hqk", queries, new_keys, preferred_element_type=jnp.float32) * factor
    )
    new_scores = new_scores - slopes[:, None, None] * new_dist[None]
    causal = (
        jnp.arange(group_size, dtype=jnp.int32)[None, :]
        <= jnp.arange(group_size, dtype=jnp.int32)[:, None]
    )
    new_scores = jnp.where(causal[None], new_scores, -jnp.inf)
    highest = jnp.maximum(
        jnp.max(cache_scores, axis=-1, keepdims=True), jnp.max(new_scores, axis=-1, keepdims=True)
    )
    cache_exp = jnp.exp(cache_scores - highest)
    new_exp = jnp.exp(new_scores - highest)
    denominator = jnp.sum(cache_exp, axis=-1, keepdims=True) + jnp.sum(
        new_exp, axis=-1, keepdims=True
    )
    cache_probs = (cache_exp / denominator).astype(jnp.bfloat16)
    new_probs = (new_exp / denominator).astype(jnp.bfloat16)
    context = jnp.einsum(
        "hqk,khd->qhd", cache_probs, cache_values, preferred_element_type=jnp.float32
    )
    context = context + jnp.einsum(
        "hqk,khd->qhd", new_probs, new_values, preferred_element_type=jnp.float32
    )
    return context.astype(jnp.bfloat16).reshape(group_size, -1)


def decode_attention(query_row, new_key, new_value, cache_keys, cache_values, length, slopes):
    factor = 1.0 / math.sqrt(query_row.shape[-1])
    cache_pos = jnp.arange(cache_keys.shape[0], dtype=jnp.int32)
    distance = (length - cache_pos).astype(jnp.float32)
    cache_scores = (
        jnp.einsum("hd,khd->hk", query_row, cache_keys, preferred_element_type=jnp.float32) * factor
    )
    cache_scores = cache_scores - slopes[:, None] * distance[None, :]
    cache_scores = jnp.where((cache_pos < length)[None, :], cache_scores, -jnp.inf)
    own_score = (
        jnp.einsum("hd,hd->h", query_row, new_key, preferred_element_type=jnp.float32)[:, None]
        * factor
    )
    highest = jnp.maximum(jnp.max(cache_scores, axis=-1, keepdims=True), own_score)
    cache_exp = jnp.exp(cache_scores - highest)
    own_exp = jnp.exp(own_score - highest)
    denominator = jnp.sum(cache_exp, axis=-1, keepdims=True) + own_exp
    cache_probs = (cache_exp / denominator).astype(jnp.bfloat16)
    own_prob = (own_exp / denominator).astype(jnp.bfloat16)
    context = jnp.einsum(
        "hk,khd->hd", cache_probs, cache_values, preferred_element_type=jnp.float32
    )
    context = context + own_prob.astype(jnp.float32) * new_value.astype(jnp.float32)
    return context.astype(jnp.bfloat16).reshape(-1)


def per_device(
    pre_hidden,
    dec_hidden,
    norm_gain,
    norm_shift,
    qkv_weight,
    qkv_bias,
    out_weight,
    out_bias,
    pre_keys,
    pre_values,
    dec_keys,
    dec_values,
    prefix_lengths,
    cache_lengths,
    slot_of,
):
    head_size = HD
    local_heads = qkv_weight.shape[1] // (3 * head_size)
    slopes = alibi_slopes(lax.axis_index("tensor") * local_heads, local_heads, H)
    bias_sum = out_bias.astype(jnp.float32)
    normed = normalize(pre_hidden, norm_gain, norm_shift)
    product = jnp.dot(
        lax.all_gather(normed, "tensor", axis=0, tiled=True),
        qkv_weight,
        preferred_element_type=jnp.float32,
    )
    merged_rows = (product + qkv_bias.astype(jnp.float32)).astype(jnp.bfloat16)
    group_size = merged_rows.shape[0]
    merged_rows = merged_rows.reshape(group_size, local_heads, 3, head_size)
    cache_size = pre_keys.shape[1]
    context = prefill_attention(
        merged_rows,
        pre_keys[0].reshape(cache_size, local_heads, head_size),
        pre_values[0].reshape(cache_size, local_heads, head_size),
        prefix_lengths[0],
        slopes,
    )
    summed = lax.psum_scatter(
        jnp.dot(context, out_weight, preferred_element_type=jnp.float32),
        "tensor",
        scatter_dimension=0,
        tiled=True,
    )
    pre_output = (summed + bias_sum + pre_hidden.astype(jnp.float32)).astype(jnp.bfloat16)
    slot_count = dec_hidden.shape[0]
    request_count = slot_of.shape[0]
    first_slot = lax.axis_index("dp") * slot_count
    slot_ids = first_slot + jnp.arange(slot_count, dtype=jnp.int32)
    slot_pick = (slot_of[None, :] == slot_ids[:, None]).astype(jnp.bfloat16)
    own_slots = lax.dynamic_slice_in_dim(slot_of, first_slot, slot_count)
    send_pick = (jnp.arange(request_count, dtype=jnp.int32)[:, None] == own_slots[None, :]).astype(
        jnp.bfloat16
    )
    gathered = lax.all_gather(dec_hidden, "dp", axis=0, tiled=True)
    arrived = jnp.dot(slot_pick, gathered, preferred_element_type=jnp.float32).astype(jnp.bfloat16)
    normed_slots = normalize(arrived, norm_gain, norm_shift)
    merged_slots = (
        jnp.dot(normed_slots, qkv_weight, preferred_element_type=jnp.float32)
        + qkv_bias.astype(jnp.float32)
    ).astype(jnp.bfloat16)
    merged_slots = merged_slots.reshape(slot_count, local_heads, 3, head_size)
    dec_cache = dec_keys.shape[1]
    slot_context = jax.vmap(decode_attention, in_axes=(0, 0, 0, 0, 0, 0, None))(
        merged_slots[:, :, 0],
        merged_slots[:, :, 1],
        merged_slots[:, :, 2],
        dec_keys.reshape(slot_count, dec_cache, local_heads, head_size),
        dec_values.reshape(slot_count, dec_cache, local_heads, head_size),
        cache_lengths,
        slopes,
    )
    slot_partial = jnp.dot(slot_context, out_weight, preferred_element_type=jnp.float32)
    slot_summed = lax.psum(slot_partial, "tensor")
    slot_rows = (slot_summed + bias_sum + arrived.astype(jnp.float32)).astype(jnp.bfloat16)
    everything = lax.all_gather(slot_rows, "dp", axis=0, tiled=True)
    dec_output = jnp.dot(send_pick.T, everything, preferred_element_type=jnp.float32).astype(
        jnp.bfloat16
    )
    return (pre_output, dec_output)


def solution(mesh):
    placed = (
        P(("dp", "tensor"), None),
        P("dp", None),
        P(),
        P(),
        P(None, "tensor"),
        P("tensor"),
        P("tensor", None),
        P(),
        P("dp", None, "tensor"),
        P("dp", None, "tensor"),
        P("dp", None, "tensor"),
        P("dp", None, "tensor"),
        P("dp"),
        P("dp"),
        P(),
    )
    return jax.shard_map(
        per_device,
        mesh=mesh,
        in_specs=placed,
        out_specs=(P(("dp", "tensor"), None), P("dp", None)),
        check_vma=False,
    )
```

profile of v0, /device:TPU:0, one launch (start us, length us, event | category | flops | bytes accessed | tf_op | source)
XLA Modules:
  0.0 207.5 jit_solution(10675507170763093559)
XLA Ops:
  7.2 0.8 convert_element_type.111
  8.1 0.7 convert_element_type.112
  8.8 1.4 convert_reduce_fusion
  10.2 1.6 fusion.11
  11.9 2.8 %fusion.14 = bf16[256,2048]{1,0:T(8,128)(2,1)} fusion(bf16[256,2048]{1,0:T(8,128)(2,1)} %param.15, f32[2048]{0:T(1024)S(1)} %convert_element_type.112, f32[2048]{0:T(1024)S(1)} %convert_element_type.111, f32[256]{0:T(256)S(1)} %add_rsqrt_fusion, f32[256]{0:T(256)S(1)} %broadcast_multiply_fusion), kind=kLoop, calls=%fused_computation.30 | loop fusion | flops 3145728 | bytes 2115584 | tf_op jit(solution)/shard_map/convert_element_type | solution.py:17
  15.4 1.3 reshape_squeeze.6
  16.7 2.3 %copy.59 = bf16[1,1024,512]{1,2,0:T(8,128)(2,1)} copy(bf16[1,1024,512]{2,1,0:T(8,128)(2,1)} %param.24) | data formatting | bytes 2097152 | tf_op jit(solution)/shard_map/reshape;squeeze | solution.py:131
  19.0 1.3 iota_compare_fusion
  20.3 3.7 %subtract_convert_fusion = (f32[1024,1024]{0,1:T(8,128)}, f32[1024,1024]{0,1:T(8,128)}) fusion(s32[1024]{0:T(1024)S(1)} %iota_add_fusion), kind=kLoop, calls=%fused_computation.14 | loop fusion | flops 4194304 | bytes 8392704 | tf_op jit(solution)/shard_map/convert_element_type | solution.py:37
  24.0 28.0 %all-gather.4.cloned.1.call-done = bf16[1024,2048]{1,0:T(8,128)(2,1)} async-done(((bf16[256,2048]{1,0:T(8,128)(2,1)}), bf16[1024,2048]{1,0:T(8,128)(2,1)}) %all-gather.4.cloned.1.call-update) | async-done | bytes 4194320 | tf_op jit(solution)/shard_map/all_gather | solution.py:120
  52.0 11.2 %add_convert_fusion = bf16[1024,1536]{1,0:T(8,128)(2,1)} fusion(bf16[1024,2048]{1,0:T(8,128)(2,1)} %all-gather.4.cloned.1.call-done, bf16[2048,1536]{1,0:T(8,128)(2,1)} %param.19, f32[1536]{0:T(1024)S(1)} %convert_element_type.114), kind=kOutput, calls=%fused_computation.10 | convolution fusion | flops 6445596672 | bytes 13637632 | tf_op jit(solution)/shard_map/dot_general | solution.py:119
  63.2 4.7 %copy.40 = bf16[1024,1536]{0,1:T(8,128)(2,1)} copy(bf16[1024,1536]{1,0:T(8,128)(2,1)} %add_convert_fusion) | data formatting | bytes 6291456 | tf_op jit(solution)/shard_map/convert_element_type | solution.py:124
  67.9 10.8 %fusion.44 = (f32[4,1024]{1,0:T(4,128)S(1)}, f32[4,1024,1024]{1,2,0:T(8,128)}) fusion(f32[1024,1024]{0,1:T(8,128)} %get-tuple-element.9, f32[4]{0:T(128)S(1)} %multiply_exponential_fusion, bf16[1024,4,3,128]{0,3,2,1:T(8,128)(2,1)} %bitcast.79, pred[1024,1024]{0,1:T(8,128)(4,1)} %iota_compare_fusion), kind=kOutput, calls=%fused_computation.86 | convolution fusion | flops 1094709248 | bytes 24133648 | tf_op jit(solution)/shard_map/qhd,khd->hqk/dot_general | solution.py:44
  78.7 3.7 %fusion.43 = (f32[4,1024]{1,0:T(4,128)S(1)}, f32[4,1024,1024]{1,2,0:T(8,128)S(1)}) fusion(f32[1024,1024]{0,1:T(8,128)S(1)} %copy-done.1, f32[4]{0:T(128)S(1)} %multiply_exponential_fusion, bf16[1024,4,3,128]{0,3,2,1:T(8,128)(2,1)S(1)} %bitcast.80, bf16[1024,4,128]{2,1,0:T(4,128)(2,1)S(1)} %reshape_squeeze.6, pred[1024]{0:T(1024)(128)(4,1)S(1)} %iota_compare_fusion.4), kind=kOutput, calls=%fused_computation.85 | convolution fusion | flops 1094709248 | bytes 23086592 | tf_op jit(solution)/shard_map/qhd,khd->hqk/dot_general | solution.py:39
  82.5 8.4 %fusion.1 = (f32[4,1024]{1,0:T(4,128)S(1)}, f32[4,1024]{1,0:T(4,128)S(1)}) fusion(f32[4,1024,1024]{1,2,0:T(8,128)} %get-tuple-element.16, f32[4,1024]{1,0:T(4,128)S(1)} %max.12, f32[4,1024,1024]{1,2,0:T(8,128)S(1)} %get-tuple-element.14), kind=kLoop, calls=%fused_computation.7 | loop fusion | flops 16769024 | bytes 33603584 | tf_op jit(solution)/shard_map/reduce_sum | solution.py:57
  90.9 3.7 %fusion.2 = f32[4,1024,128]{1,2,0:T(8,128)S(1)} fusion(bf16[1024,4,128]{0,2,1:T(8,128)(2,1)S(1)} %bitcast.82, f32[4,1024,1024]{1,2,0:T(8,128)S(1)} %get-tuple-element.14, f32[4,1024]{1,0:T(4,128)S(1)} %add.155, f32[4,1024]{1,0:T(4,128)S(1)} %max.12), kind=kOutput, calls=%fused_computation.8 | convolution fusion | flops 1086324736 | bytes 19955712 | tf_op jit(solution)/shard_map/hqk,khd->qhd/dot_general | solution.py:62
  94.6 7.7 %fusion.16 = bf16[1024,4,128]{0,2,1:T(8,128)(2,1)S(1)} fusion(f32[4,1024,128]{1,2,0:T(8,128)S(1)} %fusion.2, f32[4,1024,1024]{1,2,0:T(8,128)} %get-tuple-element.16, f32[4,1024]{1,0:T(4,128)S(1)} %add.155, f32[4,1024]{1,0:T(4,128)S(1)} %max.12, bf16[1024,4,3,128]{0,3,2,1:T(8,128)(2,1)S(1)} %bitcast.81), kind=kOutput, calls=%fused_computation.33 | convolution fusion | flops 1087373312 | bytes 21004288 | tf_op jit(solution)/shard_map/hqk,khd->qhd/dot_general | solution.py:65
  102.3 5.6 %fusion.46 = f32[1024,2048]{1,0:T(8,128)} fusion(bf16[1024,512]{0,1:T(8,128)(2,1)S(1)} %bitcast.86, bf16[512,2048]{1,0:T(8,128)(2,1)S(1)} %copy-done), kind=kOutput, calls=%fused_computation.88 | convolution fusion | flops 2147483648 | bytes 11534336 | tf_op jit(solution)/shard_map/dot_general | solution.py:136
  107.9 0.7 copy-done.7
  108.6 30.6 %all-gather = bf16[8,2,2048]{2,1,0:T(2,128)(2,1)S(1)} all-gather(bf16[1,2,2048]{2,1,0:T(2,128)(2,1)S(1)} %bitcast.84), channel_id=1, replica_groups=mesh['dp'=8,'tensor'=4] {'dp'}, dimensions={0}, use_global_device_ids=true | all-gather | bytes 73728 | tf_op jit(solution)/shard_map/all_gather | solution.py:151
  139.2 0.3 fusion.45
  139.5 0.2 multiply_reduce_fusion
  139.7 4.0 %fusion.9 = bf16[2,1536]{1,0:T(2,128)(2,1)S(1)} fusion(bf16[2048,1536]{1,0:T(8,128)(2,1)} %param.19, f32[2,2048]{1,0:T(2,128)S(1)} %get-tuple-element.18, f32[2]{0:T(128)S(1)} %add_rsqrt_fusion.1, f32[2]{0:T(128)S(1)} %broadcast_multiply_fusion.1, f32[2048]{0:T(1024)S(1)} %convert_element_type.112, f32[2048]{0:T(1024)S(1)} %convert_element_type.111, ...), kind=kOutput, calls=%fused_computation.23 | convolution fusion | flops 12609536 | bytes 6336528 | tf_op jit(solution)/shard_map/dot_general | solution.py:155
  143.8 6.3 %copy.60 = bf16[2,2048,512]{1,2,0:T(8,128)(2,1)} copy(bf16[2,2048,512]{2,1,0:T(8,128)(2,1)} %param.25) | data formatting | bytes 8388608 | tf_op jit(solution)/shard_map/reshape | solution.py:164
  150.2 3.2 %fusion.28 = f32[2,4,1,2048]{3,2,1,0:T(1,128)S(1)} fusion(bf16[2,2048,4,128]{1,3,2,0:T(8,128)(2,1)} %bitcast.78, bf16[2,4,3,128]{3,2,1,0:T(4,128)(2,1)S(1)} %reshape.204), kind=kOutput, calls=%fused_computation.59 | convolution fusion | flops 4194304 | bytes 4263936 | tf_op jit(solution)/shard_map/vmap(hd,khd->hk)/dot_general | solution.py:76
  153.8 0.2 fusion.21
  154.1 0.7 fusion.4
  154.8 0.4 fusion.32
  155.2 11.1 %psum.7 = f32[2,2048]{1,0:T(2,128)S(1)} all-reduce(f32[2,2048]{1,0:T(2,128)S(1)} %fusion.32), channel_id=1, replica_groups=mesh['dp'=8,'tensor'=4] {'tensor'}, use_global_device_ids=true, to_apply=%region_11.12 | all-reduce | flops 4096 | bytes 32768 | tf_op jit(solution)/shard_map/psum | solution.py:170
  166.4 30.5 %all-gather.1 = bf16[8,2,2048]{2,1,0:T(2,128)(2,1)S(1)} all-gather(bf16[1,2,2048]{2,1,0:T(2,128)(2,1)S(1)} %fusion.24), channel_id=1, replica_groups=mesh['dp'=8,'tensor'=4] {'dp'}, dimensions={0}, use_global_device_ids=true | all-gather | bytes 73728 | tf_op jit(solution)/shard_map/all_gather | solution.py:172
  197.0 0.8 convolution_convert_fusion
  197.8 2.9 %fusion.15 = bf16[256,2048]{1,0:T(8,128)(2,1)} fusion(bf16[256,2048]{1,0:T(8,128)(2,1)S(1)} %copy-done.2, f32[256,2048]{1,0:T(8,128)} %reduce-scatter.2.cloned.1.call-done, f32[2048]{0:T(1024)S(1)} %convert_element_type.122), kind=kLoop, calls=%fused_computation.31 | loop fusion | flops 2097152 | bytes 4202496 | tf_op jit(solution)/shard_map/convert_element_type | solution.py:141
  (52 shorter events, 1.1 us)
Async XLA Ops:
  7.2 95.1 %copy-start = (bf16[512,2048]{1,0:T(8,128)(2,1)S(1)}, bf16[512,2048]{1,0:T(8,128)(2,1)}, u32[]{:S(2)}) copy-start(bf16[512,2048]{1,0:T(8,128)(2,1)} %param.21) | copy-start | bytes 6291460
  7.2 7.5 %copy-start.6 = (bf16[1536]{0:T(1024)(128)(2,1)S(1)}, bf16[1536]{0:T(1024)(128)(2,1)}, u32[]{:S(2)}) copy-start(bf16[1536]{0:T(1024)(128)(2,1)} %param.20) | copy-start | bytes 9220
  7.2 44.8 %all-gather.4.cloned.1.call-start = ((), (), s32[]{:S(2)}) async-start(), calls=%async_computation.1 | async-start | bytes 5242880 | tf_op jit(solution)/shard_map/all_gather | solution.py:120
  14.6 183.1 %reduce-scatter.2.cloned.1.call-start = ((), (), s32[]{:S(2)}) async-start(), calls=%async_computation.2 | async-start | bytes 10485760 | tf_op jit(solution)/shard_map/reduce_scatter | solution.py:135
  67.9 10.9 %copy-start.1 = (f32[1024,1024]{0,1:T(8,128)S(1)}, f32[1024,1024]{0,1:T(8,128)}, u32[]{:S(2)}) copy-start(f32[1024,1024]{0,1:T(8,128)} %get-tuple-element.10) | copy-start | bytes 12582916
  67.9 10.9 %copy-start.3 = (bf16[1024,1536]{0,1:T(8,128)(2,1)S(1)}, bf16[1024,1536]{0,1:T(8,128)(2,1)}, u32[]{:S(2)}) copy-start(bf16[1024,1536]{0,1:T(8,128)(2,1)} %copy.40) | copy-start | bytes 9437188
  82.4 8.4 %copy-start.4 = (bf16[1,1024,512]{1,2,0:T(8,128)(2,1)S(1)}, bf16[1,1024,512]{1,2,0:T(8,128)(2,1)}, u32[]{:S(2)}) copy-start(bf16[1,1024,512]{1,2,0:T(8,128)(2,1)} %copy.59) | copy-start | bytes 3145732
  107.9 0.7 copy-start.7
  107.9 0.7 copy-start.5
  107.9 31.3 %copy-start.10 = (s32[16]{0:T(128)S(1)}, s32[16]{0:T(128)}, u32[]{:S(2)}) copy-start(s32[16]{0:T(128)} %param.29) | copy-start | bytes 196
  150.1 3.3 %copy-start.8 = (s32[2]{0:T(128)S(1)}, s32[2]{0:T(128)}, u32[]{:S(2)}) copy-start(s32[2]{0:T(128)} %param.28) | copy-start | bytes 28
  150.1 4.0 %copy-start.9 = (bf16[2,2048,512]{2,1,0:T(8,128)(2,1)S(1)}, bf16[2,2048,512]{2,1,0:T(8,128)(2,1)}, u32[]{:S(2)}) copy-start(bf16[2,2048,512]{2,1,0:T(8,128)(2,1)} %param.26) | copy-start | bytes 12582916
  153.4 44.4 %copy-start.2 = (bf16[256,2048]{1,0:T(8,128)(2,1)S(1)}, bf16[256,2048]{1,0:T(8,128)(2,1)}, u32[]{:S(2)}) copy-start(bf16[256,2048]{1,0:T(8,128)(2,1)} %param.15) | copy-start | bytes 3145732
Sparse Core Ops, SparseCore 0:
  14.8 37.1 all-gather.3
  108.0 71.9 reduce-scatter.1
where the time goes:
time: 208 us; the launch traced here: 207 us
  blocking collectives  72.2 us (35%)
  matrix products  52.1 us (25%)
  waiting for transfers between devices  28 us (13%)
  other arithmetic  24.7 us (12%)
  local copies, waits for them, and re-layouts  15.5 us (7%)
  between operations  14.9 us (7%)
    all_gather x1, blocking collectives, per_device(): gathered = lax.all_gather(dec_hidden, 'dp', axis=0, tiled=True)  30.6 us
    all_gather x1, blocking collectives, per_device(): everything = lax.all_gather(slot_rows, 'dp', axis=0, tiled=True)  30.5 us
    all_gather x1, waiting for transfers between devices, per_device(): lax.all_gather(normed, 'tensor', axis=0, tiled=True)  28 us
    dot_general x1, matrix products, per_device(): jnp.dot(lax.all_gather(normed, 'tensor', axis=0, tiled=True), qkv_weight,...  11.2 us
    psum x1, blocking collectives, per_device(): slot_summed = lax.psum(slot_partial, 'tensor')  11.1 us
    dot_general x1, matrix products, prefill_attention(): jnp.einsum('qhd,khd->hqk', queries, new_keys, preferred_element_type=jnp....  10.8 us
    reduce_sum x1, other arithmetic, prefill_attention(): jnp.sum(new_exp, axis=-1, keepdims=True)  8.4 us
    dot_general x1, matrix products, prefill_attention(): jnp.einsum('hqk,khd->qhd', new_probs, new_values, preferred_element_type=...  7.69 us
  transfers between devices with their start and end apart: 2, of which 1 were waited for; matrix products, arithmetic and copies ran while one was open for 12% of the time, Pallas kernels for 0%

commit v1 on v0

--- a/solution.py
+++ b/solution.py
@@ -167,7 +167,7 @@
         slopes,
     )
     slot_partial = jnp.dot(slot_context, out_weight, preferred_element_type=jnp.float32)
-    slot_summed = lax.psum(slot_partial, "tensor")
+    slot_summed = jnp.sum(lax.all_gather(slot_partial, "tensor"), axis=0)
     slot_rows = (slot_summed + bias_sum + arrived.astype(jnp.float32)).astype(jnp.bfloat16)
     everything = lax.all_gather(slot_rows, "dp", axis=0, tiled=True)
     dec_output = jnp.dot(send_pick.T, everything, preferred_element_type=jnp.float32).astype(

time: 208 us -> 203 us (0.976)
  blocking collectives: 72.2 us -> 66.6 us
    psum x1 -> x0, blocking collectives: 11.1 us -> none  [per_device(): slot_summed = lax.psum(slot_partial, 'tensor')]
    all_gather x0 -> x1, blocking collectives: none -> 5.56 us  [per_device(): slot_summed = jnp.sum(lax.all_gather(slot_partial, 'tensor'), axis=0)]
  transfers between devices with their start and end apart: 2 -> 2, of which waited for: 1 -> 1; matrix products, arithmetic and copies ran while one was open for 12% -> 13% of each run, Pallas kernels for 0% -> 0%
where the time goes in v1:
time: 203 us; the launch traced here: 202 us
  blocking collectives  66.6 us (33%)
  matrix products  52.1 us (26%)
  waiting for transfers between devices  28 us (14%)
  other arithmetic  24.7 us (12%)
  local copies, waits for them, and re-layouts  15.5 us (8%)
  between operations  14.9 us (7%)
    all_gather x1, blocking collectives, per_device(): gathered = lax.all_gather(dec_hidden, 'dp', axis=0, tiled=True)  30.6 us
    all_gather x1, blocking collectives, per_device(): everything = lax.all_gather(slot_rows, 'dp', axis=0, tiled=True)  30.5 us
    all_gather x1, waiting for transfers between devices, per_device(): lax.all_gather(normed, 'tensor', axis=0, tiled=True)  28 us
    dot_general x1, matrix products, per_device(): jnp.dot(lax.all_gather(normed, 'tensor', axis=0, tiled=True), qkv_weight,...  11.2 us
    dot_general x1, matrix products, prefill_attention(): jnp.einsum('qhd,khd->hqk', queries, new_keys, preferred_element_type=jnp....  10.8 us
    reduce_sum x1, other arithmetic, prefill_attention(): jnp.sum(new_exp, axis=-1, keepdims=True)  8.4 us
    dot_general x1, matrix products, prefill_attention(): jnp.einsum('hqk,khd->qhd', new_probs, new_values, preferred_element_type=...  7.69 us
    reshape x1, local copies, waits for them, and re-layouts, per_device(): dec_keys.reshape(slot_count, dec_cache, local_heads, head_size)  6.31 us
  transfers between devices with their start and end apart: 2, of which 1 were waited for; matrix products, arithmetic and copies ran while one was open for 13% of the time, Pallas kernels for 0%

profile of v1, /device:TPU:0, one launch (start us, length us, event | category | flops | bytes accessed | tf_op | source)
XLA Modules:
  0.0 202.0 jit_solution(16831610453844583385)
XLA Ops:
  7.2 0.8 convert_element_type.111
  8.1 0.7 convert_element_type.112
  8.8 1.4 convert_reduce_fusion
  10.2 1.6 fusion.11
  11.9 2.8 %fusion.14 = bf16[256,2048]{1,0:T(8,128)(2,1)} fusion(bf16[256,2048]{1,0:T(8,128)(2,1)} %param.15, f32[2048]{0:T(1024)S(1)} %convert_element_type.112, f32[2048]{0:T(1024)S(1)} %convert_element_type.111, f32[256]{0:T(256)S(1)} %add_rsqrt_fusion, f32[256]{0:T(256)S(1)} %broadcast_multiply_fusion), kind=kLoop, calls=%fused_computation.31 | loop fusion | flops 3145728 | bytes 2115584 | tf_op jit(solution)/shard_map/convert_element_type | solution.py:17
  15.4 1.3 reshape_squeeze.6
  16.7 2.3 %copy.59 = bf16[1,1024,512]{1,2,0:T(8,128)(2,1)} copy(bf16[1,1024,512]{2,1,0:T(8,128)(2,1)} %param.24) | data formatting | bytes 2097152 | tf_op jit(solution)/shard_map/reshape;squeeze | solution.py:131
  19.0 1.3 iota_compare_fusion
  20.3 3.7 %subtract_convert_fusion = (f32[1024,1024]{0,1:T(8,128)}, f32[1024,1024]{0,1:T(8,128)}) fusion(s32[1024]{0:T(1024)S(1)} %iota_add_fusion), kind=kLoop, calls=%fused_computation.14 | loop fusion | flops 4194304 | bytes 8392704 | tf_op jit(solution)/shard_map/convert_element_type | solution.py:37
  24.0 28.0 %all-gather.6.cloned.1.call-done = bf16[1024,2048]{1,0:T(8,128)(2,1)} async-done(((bf16[256,2048]{1,0:T(8,128)(2,1)}), bf16[1024,2048]{1,0:T(8,128)(2,1)}) %all-gather.6.cloned.1.call-update) | async-done | bytes 4194320 | tf_op jit(solution)/shard_map/all_gather | solution.py:120
  52.0 11.2 %add_convert_fusion = bf16[1024,1536]{1,0:T(8,128)(2,1)} fusion(bf16[1024,2048]{1,0:T(8,128)(2,1)} %all-gather.6.cloned.1.call-done, bf16[2048,1536]{1,0:T(8,128)(2,1)} %param.19, f32[1536]{0:T(1024)S(1)} %convert_element_type.114), kind=kOutput, calls=%fused_computation.10 | convolution fusion | flops 6445596672 | bytes 13637632 | tf_op jit(solution)/shard_map/dot_general | solution.py:119
  63.2 4.7 %copy.40 = bf16[1024,1536]{0,1:T(8,128)(2,1)} copy(bf16[1024,1536]{1,0:T(8,128)(2,1)} %add_convert_fusion) | data formatting | bytes 6291456 | tf_op jit(solution)/shard_map/convert_element_type | solution.py:124
  67.9 10.8 %fusion.43 = (f32[4,1024]{1,0:T(4,128)S(1)}, f32[4,1024,1024]{1,2,0:T(8,128)}) fusion(f32[1024,1024]{0,1:T(8,128)} %get-tuple-element.9, f32[4]{0:T(128)S(1)} %multiply_exponential_fusion, bf16[1024,4,3,128]{0,3,2,1:T(8,128)(2,1)} %bitcast.81, pred[1024,1024]{0,1:T(8,128)(4,1)} %iota_compare_fusion), kind=kOutput, calls=%fused_computation.86 | convolution fusion | flops 1094709248 | bytes 24133648 | tf_op jit(solution)/shard_map/qhd,khd->hqk/dot_general | solution.py:44
  78.7 3.7 %fusion.42 = (f32[4,1024]{1,0:T(4,128)S(1)}, f32[4,1024,1024]{1,2,0:T(8,128)S(1)}) fusion(f32[1024,1024]{0,1:T(8,128)S(1)} %copy-done.1, f32[4]{0:T(128)S(1)} %multiply_exponential_fusion, bf16[1024,4,3,128]{0,3,2,1:T(8,128)(2,1)S(1)} %bitcast.82, bf16[1024,4,128]{2,1,0:T(4,128)(2,1)S(1)} %reshape_squeeze.6, pred[1024]{0:T(1024)(128)(4,1)S(1)} %iota_compare_fusion.4), kind=kOutput, calls=%fused_computation.85 | convolution fusion | flops 1094709248 | bytes 23086592 | tf_op jit(solution)/shard_map/qhd,khd->hqk/dot_general | solution.py:39
  82.5 8.4 %fusion.1 = (f32[4,1024]{1,0:T(4,128)S(1)}, f32[4,1024]{1,0:T(4,128)S(1)}) fusion(f32[4,1024,1024]{1,2,0:T(8,128)} %get-tuple-element.16, f32[4,1024]{1,0:T(4,128)S(1)} %max.12, f32[4,1024,1024]{1,2,0:T(8,128)S(1)} %get-tuple-element.14), kind=kLoop, calls=%fused_computation.7 | loop fusion | flops 16769024 | bytes 33603584 | tf_op jit(solution)/shard_map/reduce_sum | solution.py:57
  90.9 3.7 %fusion.2 = f32[4,1024,128]{1,2,0:T(8,128)S(1)} fusion(bf16[1024,4,128]{0,2,1:T(8,128)(2,1)S(1)} %bitcast.84, f32[4,1024,1024]{1,2,0:T(8,128)S(1)} %get-tuple-element.14, f32[4,1024]{1,0:T(4,128)S(1)} %add.153, f32[4,1024]{1,0:T(4,128)S(1)} %max.12), kind=kOutput, calls=%fused_computation.8 | convolution fusion | flops 1086324736 | bytes 19955712 | tf_op jit(solution)/shard_map/hqk,khd->qhd/dot_general | solution.py:62
  94.6 7.7 %fusion.16 = bf16[1024,4,128]{0,2,1:T(8,128)(2,1)S(1)} fusion(f32[4,1024,128]{1,2,0:T(8,128)S(1)} %fusion.2, f32[4,1024,1024]{1,2,0:T(8,128)} %get-tuple-element.16, f32[4,1024]{1,0:T(4,128)S(1)} %add.153, f32[4,1024]{1,0:T(4,128)S(1)} %max.12, bf16[1024,4,3,128]{0,3,2,1:T(8,128)(2,1)S(1)} %bitcast.83), kind=kOutput, calls=%fused_computation.34 | convolution fusion | flops 1087373312 | bytes 21004288 | tf_op jit(solution)/shard_map/hqk,khd->qhd/dot_general | solution.py:65
  102.3 5.6 %fusion.45 = f32[1024,2048]{1,0:T(8,128)} fusion(bf16[1024,512]{0,1:T(8,128)(2,1)S(1)} %bitcast.88, bf16[512,2048]{1,0:T(8,128)(2,1)S(1)} %copy-done), kind=kOutput, calls=%fused_computation.88 | convolution fusion | flops 2147483648 | bytes 11534336 | tf_op jit(solution)/shard_map/dot_general | solution.py:136
  107.9 0.7 copy-done.7
  108.6 30.6 %all-gather.1 = bf16[8,2,2048]{2,1,0:T(2,128)(2,1)S(1)} all-gather(bf16[1,2,2048]{2,1,0:T(2,128)(2,1)S(1)} %bitcast.86), channel_id=1, replica_groups=mesh['dp'=8,'tensor'=4] {'dp'}, dimensions={0}, use_global_device_ids=true | all-gather | bytes 73728 | tf_op jit(solution)/shard_map/all_gather | solution.py:151
  139.2 0.3 fusion.44
  139.5 0.2 multiply_reduce_fusion
  139.7 4.0 %fusion.9 = bf16[2,1536]{1,0:T(2,128)(2,1)S(1)} fusion(bf16[2048,1536]{1,0:T(8,128)(2,1)} %param.19, f32[2,2048]{1,0:T(2,128)S(1)} %get-tuple-element.18, f32[2]{0:T(128)S(1)} %add_rsqrt_fusion.1, f32[2]{0:T(128)S(1)} %broadcast_multiply_fusion.1, f32[2048]{0:T(1024)S(1)} %convert_element_type.112, f32[2048]{0:T(1024)S(1)} %convert_element_type.111, ...), kind=kOutput, calls=%fused_computation.24 | convolution fusion | flops 12609536 | bytes 6336528 | tf_op jit(solution)/shard_map/dot_general | solution.py:155
  143.8 6.3 %copy.60 = bf16[2,2048,512]{1,2,0:T(8,128)(2,1)} copy(bf16[2,2048,512]{2,1,0:T(8,128)(2,1)} %param.25) | data formatting | bytes 8388608 | tf_op jit(solution)/shard_map/reshape | solution.py:164
  150.2 3.2 %fusion.28 = f32[2,4,1,2048]{3,2,1,0:T(1,128)S(1)} fusion(bf16[2,2048,4,128]{1,3,2,0:T(8,128)(2,1)} %bitcast.80, bf16[2,4,3,128]{3,2,1,0:T(4,128)(2,1)S(1)} %reshape.204), kind=kOutput, calls=%fused_computation.60 | convolution fusion | flops 4194304 | bytes 4263936 | tf_op jit(solution)/shard_map/vmap(hd,khd->hk)/dot_general | solution.py:76
  153.8 0.2 fusion.21
  154.1 0.7 fusion.4
  154.8 0.4 convolution_bitcast_fusion
  155.2 5.6 %all-gather.2 = f32[4,2,2048]{2,1,0:T(2,128)S(1)} all-gather(f32[1,2,2048]{2,1,0:T(2,128)S(1)} %convolution_bitcast_fusion), channel_id=2, replica_groups=mesh['dp'=8,'tensor'=4] {'tensor'}, dimensions={0}, use_global_device_ids=true | all-gather | bytes 81920 | tf_op jit(solution)/shard_map/all_gather | solution.py:170
  160.8 30.5 %all-gather.3 = bf16[8,2,2048]{2,1,0:T(2,128)(2,1)S(1)} all-gather(bf16[1,2,2048]{2,1,0:T(2,128)(2,1)S(1)} %fusion.24), channel_id=1, replica_groups=mesh['dp'=8,'tensor'=4] {'dp'}, dimensions={0}, use_global_device_ids=true | all-gather | bytes 73728 | tf_op jit(solution)/shard_map/all_gather | solution.py:172
  191.4 0.8 convolution_convert_fusion
  192.2 2.9 %fusion.15 = bf16[256,2048]{1,0:T(8,128)(2,1)} fusion(bf16[256,2048]{1,0:T(8,128)(2,1)S(1)} %copy-done.2, f32[256,2048]{1,0:T(8,128)} %reduce-scatter.2.cloned.1.call-done, f32[2048]{0:T(1024)S(1)} %convert_element_type.122), kind=kLoop, calls=%fused_computation.32 | loop fusion | flops 2097152 | bytes 4202496 | tf_op jit(solution)/shard_map/convert_element_type | solution.py:141
  (53 shorter events, 1.1 us)
Async XLA Ops:
  7.2 95.1 %copy-start = (bf16[512,2048]{1,0:T(8,128)(2,1)S(1)}, bf16[512,2048]{1,0:T(8,128)(2,1)}, u32[]{:S(2)}) copy-start(bf16[512,2048]{1,0:T(8,128)(2,1)} %param.21) | copy-start | bytes 6291460
  7.2 7.5 %copy-start.6 = (bf16[1536]{0:T(1024)(128)(2,1)S(1)}, bf16[1536]{0:T(1024)(128)(2,1)}, u32[]{:S(2)}) copy-start(bf16[1536]{0:T(1024)(128)(2,1)} %param.20) | copy-start | bytes 9220
  7.2 44.8 %all-gather.6.cloned.1.call-start = ((), (), s32[]{:S(2)}) async-start(), calls=%async_computation.1 | async-start | bytes 5242880 | tf_op jit(solution)/shard_map/all_gather | solution.py:120
  14.6 177.6 %reduce-scatter.2.cloned.1.call-start = ((), (), s32[]{:S(2)}) async-start(), calls=%async_computation.2 | async-start | bytes 10485760 | tf_op jit(solution)/shard_map/reduce_scatter | solution.py:135
  67.9 10.9 %copy-start.1 = (f32[1024,1024]{0,1:T(8,128)S(1)}, f32[1024,1024]{0,1:T(8,128)}, u32[]{:S(2)}) copy-start(f32[1024,1024]{0,1:T(8,128)} %get-tuple-element.10) | copy-start | bytes 12582916
  67.9 10.9 %copy-start.3 = (bf16[1024,1536]{0,1:T(8,128)(2,1)S(1)}, bf16[1024,1536]{0,1:T(8,128)(2,1)}, u32[]{:S(2)}) copy-start(bf16[1024,1536]{0,1:T(8,128)(2,1)} %copy.40) | copy-start | bytes 9437188
  82.4 8.4 %copy-start.4 = (bf16[1,1024,512]{1,2,0:T(8,128)(2,1)S(1)}, bf16[1,1024,512]{1,2,0:T(8,128)(2,1)}, u32[]{:S(2)}) copy-start(bf16[1,1024,512]{1,2,0:T(8,128)(2,1)} %copy.59) | copy-start | bytes 3145732
  107.9 0.7 copy-start.7
  107.9 0.7 copy-start.5
  107.9 31.3 %copy-start.10 = (s32[16]{0:T(128)S(1)}, s32[16]{0:T(128)}, u32[]{:S(2)}) copy-start(s32[16]{0:T(128)} %param.29) | copy-start | bytes 196
  150.1 3.3 %copy-start.8 = (s32[2]{0:T(128)S(1)}, s32[2]{0:T(128)}, u32[]{:S(2)}) copy-start(s32[2]{0:T(128)} %param.28) | copy-start | bytes 28
  150.1 4.0 %copy-start.9 = (bf16[2,2048,512]{2,1,0:T(8,128)(2,1)S(1)}, bf16[2,2048,512]{2,1,0:T(8,128)(2,1)}, u32[]{:S(2)}) copy-start(bf16[2,2048,512]{2,1,0:T(8,128)(2,1)} %param.26) | copy-start | bytes 12582916
  153.4 38.8 %copy-start.2 = (bf16[256,2048]{1,0:T(8,128)(2,1)S(1)}, bf16[256,2048]{1,0:T(8,128)(2,1)}, u32[]{:S(2)}) copy-start(bf16[256,2048]{1,0:T(8,128)(2,1)} %param.15) | copy-start | bytes 3145732
Sparse Core Ops, SparseCore 0:
  14.8 37.1 all-gather.5
  108.0 72.0 reduce-scatter.1
